TPU v7x, 256 devices: a whole 4x4x8 slice. The times are simulated.
256 devices in a mesh: dom: 64 (over y, z, core), rep: 4 (over x).
Axes of the slice: x: 4, y: 4, z: 8, core: 2. Of those that a mesh axis runs over, the one named last changes fastest.
Arguments:
- x_loader: bfloat16 [131072, 512], P(('dom', 'rep')), may hold values from -6 to 6
- owner_index: int32 [131072], P(('dom', 'rep')), may hold values from 0 to 131071, as said below
- tile_vals: bfloat16 [1024, 12, 128, 128], P(('dom', 'rep')), as said below
- tile_cols: int32 [1024, 12], P(('dom', 'rep')), may hold values from 0 to 1023, as said below
- tile_live: int32 [1024, 12], P(('dom', 'rep')), may hold values from 0 to 1, as said below
- w_self: bfloat16 [512, 512], replicated, may hold values from -0.25 to 0.25
- w_neigh: bfloat16 [512, 512], replicated, may hold values from -3 to 3
- bias: float32 [512], replicated, may hold values from -3 to 3
- cotangent: bfloat16 [131072, 512], P(('dom', 'rep')), may hold values from -6 to 6
Outputs:
- layer_out: bfloat16 [131072, 512], P(('dom', 'rep'))
- grad_features: bfloat16 [131072, 512], P(('dom', 'rep'))
- grad_self: float32 [512, 512], replicated
- grad_neigh: float32 [512, 512], replicated
- grad_bias: float32 [512], replicated
Inputs may be any that keep to these rules, and one draw needn't show every extreme that they name: `owner_index`: A permutation of the 131072 rows. Loader rows are in blocks of 512 in the order of the devices (dom slowest); owner rows likewise. The 512 rows of each loader block with rep index r go to owner blocks of rep index r, 8 rows to each of the 64 partitions. `tile_cols`: partition p holds row tiles p * 16 to (p + 1) * 16 - 1. A column tile of a row tile of partition p lies in partition p or within 4 tiles beyond its edges. W is symmetric: every live slot (t, c) with tiles B is matched by a live slot (c, t) with tiles B^T, a slot with c = t holding a symmetric tile. `tile_live`: live slots are symmetric as stated for tile_cols. `tile_vals`: nonnegative edge weights.
All inputs are finite; a program needn't handle non-finite values.
Results may differ from a plain program's by a relative error of at most 0.0075.
Values may be sent and summed in bfloat16 or wider, within the bound.
No kernel may reach another device: no remote copies, remote signals or barrier semaphores. Data moves between devices by JAX's collectives and lax.ppermute only.
A program may use at most 64 MiB of HBM per device.

v0:
```python
import jax
import jax.numpy as jnp
from jax import lax
from jax.sharding import PartitionSpec as P

HALO_T = 4


def shifted(value, axis, steps):
    count = lax.axis_size(axis)
    first, last = (max(0, -steps), min(count, count - steps))
    return lax.ppermute(value, axis, [(source, source + steps) for source in range(first, last)])


def with_halo(block, sides, width):
    for axis, dim in sides:
        count = lax.axis_size(axis)
        forward = [(i, i + 1) for i in range(count - 1)]
        backward = [(target, source) for source, target in forward]
        low = lax.ppermute(
            lax.slice_in_dim(block, block.shape[dim] - width, None, axis=dim), axis, forward
        )
        high = lax.ppermute(lax.slice_in_dim(block, 0, width, axis=dim), axis, backward)
        block = jnp.concatenate([low, block, high], axis=dim)
    return block


def contract_rows(left, right):
    return lax.dot_general(
        left, right, (((0,), (0,)), ((), ())), preferred_element_type=jnp.float32
    )


def contract_cols(left, right):
    return lax.dot_general(
        left, right, (((1,), (1,)), ((), ())), preferred_element_type=jnp.float32
    )


def pass_rim(values, offset):
    return shifted(values.astype(jnp.bfloat16), "dom", offset).astype(values.dtype)


def shards(
    x_loader, owner_index, tile_vals, tile_cols, tile_live, w_self, w_neigh, bias, cotangent
):
    rows, width = x_loader.shape
    reps = lax.axis_size("rep")
    dom_place = lax.axis_index("dom")
    part_rows = rows * reps
    part_tiles = part_rows // 128
    row_tiles = rows // 128
    rim_rows = HALO_T * 128
    dest = owner_index // part_rows
    order = jnp.argsort(dest, stable=True)
    moved, slot = (
        lax.all_to_all(x_loader[order], "dom", split_axis=0, concat_axis=0, tiled=True),
        lax.all_to_all((owner_index % rows)[order], "dom", split_axis=0, concat_axis=0, tiled=True),
    )
    features = jnp.zeros((rows, width), jnp.bfloat16).at[slot].set(moved)
    first_tile = dom_place * part_tiles - HALO_T
    local_cols = tile_cols - first_tile
    masked = tile_vals * tile_live.astype(jnp.bfloat16)[:, :, None, None]
    degree = 1.0 + jnp.sum(masked, axis=(1, 3), dtype=jnp.float32)
    whole = lax.all_gather(features, "rep", axis=0, tiled=True)
    extended = with_halo(whole, (("dom", 0),), rim_rows)
    picked = extended.reshape(-1, 128, width)[local_cols]
    summed = jnp.einsum("tkab,tkbf->taf", masked, picked, preferred_element_type=jnp.float32)
    agg = (summed / degree[:, :, None]).reshape(rows, width).astype(jnp.bfloat16)
    pre = (
        jnp.dot(features, w_self, preferred_element_type=jnp.float32)
        + jnp.dot(agg, w_neigh, preferred_element_type=jnp.float32)
        + bias
    )
    layer_out = jnp.where(pre > 0, pre, jnp.expm1(jnp.minimum(pre, 0.0))).astype(jnp.bfloat16)
    slope = jnp.where(pre > 0, 1.0, jnp.exp(jnp.minimum(pre, 0.0)))
    dz = (cotangent.astype(jnp.float32) * slope).astype(jnp.bfloat16)
    grad_self, grad_neigh, grad_bias = lax.psum(
        (
            contract_rows(features, dz),
            contract_rows(agg, dz),
            jnp.sum(dz, axis=0, dtype=jnp.float32),
        ),
        ("dom", "rep"),
    )
    scaled = (contract_cols(dz, w_neigh) / degree.reshape(rows, 1)).astype(jnp.bfloat16)
    terms = jnp.einsum(
        "tkab,taf->tkbf",
        masked,
        scaled.reshape(row_tiles, 128, width),
        preferred_element_type=jnp.float32,
    )
    span_tiles = part_tiles + 2 * HALO_T
    selector = (
        local_cols.reshape(-1)[None, :] == jnp.arange(span_tiles, dtype=jnp.int32)[:, None]
    ).astype(jnp.float32)
    buffer = jnp.einsum(
        "en,nbf->ebf", selector, terms.reshape(-1, 128, width), precision=lax.Precision.HIGHEST
    )
    buffer = buffer.reshape(span_tiles * 128, width)
    lower = buffer[:rim_rows]
    upper = buffer[rim_rows + part_rows :]
    core = buffer[rim_rows : rim_rows + part_rows]
    core = core.at[:rim_rows].add(pass_rim(upper, 1))
    core = core.at[part_rows - rim_rows :].add(pass_rim(lower, -1))
    back = lax.psum_scatter(core, "rep", scatter_dimension=0, tiled=True)
    grad_features = (contract_cols(dz, w_self) + back).astype(jnp.bfloat16)
    return (layer_out, grad_features, grad_self, grad_neigh, grad_bias)


def solution(mesh):
    return jax.shard_map(
        shards,
        mesh=mesh,
        in_specs=(
            P(("dom", "rep"), None),
            P(("dom", "rep")),
            P(("dom", "rep"), None, None, None),
            P(("dom", "rep"), None),
            P(("dom", "rep"), None),
            P(),
            P(),
            P(),
            P(("dom", "rep"), None),
        ),
        out_specs=(P(("dom", "rep"), None), P(("dom", "rep"), None), P(), P(), P()),
        check_vma=False,
    )
```

profile of v0, /device:TPU:2, one launch (start us, length us, event | category | flops | bytes accessed | tf_op | source)
XLA Modules:
  0.0 486.7 jit_solution(7837561082085686232)
XLA Ops:
  8.0 3.8 sort.17
  11.8 3.5 gather_fusion
  16.0 12.1 %all-to-all-start = ((s32[64,8,1]{1,2,0:T(1,128)}), s32[64,8,1]{1,2,0:T(1,128)S(1)}, u32[]{:S(2)}, u32[]{:S(2)}) async-start(s32[64,8,1]{1,2,0:T(1,128)} %bitcast), calls=%async_computation | async-start | bytes 65536 | tf_op jit(solution)/shard_map/all_to_all | solution.py:58
  28.1 2.6 gather_fusion.1
  30.7 6.8 %all-to-all-done = s32[64,8,1]{1,2,0:T(1,128)S(1)} async-done(((s32[64,8,1]{1,2,0:T(1,128)}), s32[64,8,1]{1,2,0:T(1,128)S(1)}, u32[]{:S(2)}, u32[]{:S(2)}) %all-to-all-start) | async-done | bytes 2080 | tf_op jit(solution)/shard_map/all_to_all | solution.py:58
  37.5 4.6 all-to-all-start.1
  43.6 15.8 %all-to-all-done.1 = bf16[64,8,512]{2,1,0:T(8,128)(2,1)S(1)} async-done(((bf16[64,8,512]{2,1,0:T(8,128)(2,1)}), bf16[64,8,512]{2,1,0:T(8,128)(2,1)S(1)}, u32[]{:S(2)}, u32[]{:S(2)}) %all-to-all-start.1) | async-done | bytes 524320 | tf_op jit(solution)/shard_map/all_to_all | solution.py:57
  59.4 3.2 scatter_custom_fusion
  63.2 29.2 %all-gather.2.cloned.1.call-done = bf16[2048,512]{1,0:T(8,128)(2,1)} async-done(((bf16[512,512]{1,0:T(8,128)(2,1)}), bf16[2048,512]{1,0:T(8,128)(2,1)}) %all-gather.2.cloned.1.call-update) | async-done | bytes 2097168 | tf_op jit(solution)/shard_map/all_gather | solution.py:65
  92.4 2.2 fusion.26
  94.6 2.5 collective-permute-start
  101.9 3.1 pad_maximum_fusion
  105.0 6.8 %gather_fusion.2 = bf16[48,128,512]{2,1,0:T(8,128)(2,1)} fusion(bf16[24,128,512]{2,1,0:T(8,128)(2,1)} %bitcast.50, s32[1024]{0:T(1024)S(1)} %pad_clamp_fusion), kind=kCustom, calls=%fused_computation.2 | custom fusion | bytes 12583104 | tf_op jit(solution)/shard_map/gather | solution.py:67
  111.9 4.0 fusion.5
  118.1 1.9 fusion.6
  120.1 12.3 %fusion.27 = (bf16[24,128,512]{2,0,1:T(8,128)(2,1)S(1)}, f32[24,128,512]{2,0,1:T(8,128)S(1)}) fusion(f32[48,128,512]{2,1,0:T(8,128)S(1)} %bitcast.49, s32[48]{0:T(128)S(1)} %eq.17), kind=kOutput, calls=%fused_computation.56 | convolution fusion | flops 907543680 | bytes 22020288 | tf_op jit(solution)/shard_map/en,nbf->ebf/dot_general | solution.py:97
  132.9 9.1 %collective-permute-start.2 = (bf16[512,512]{1,0:T(8,128)(2,1)S(1)}, bf16[512,512]{1,0:T(8,128)(2,1)S(1)}, u32[]{:S(2)}, u32[]{:S(2)}) collective-permute-start(bf16[512,512]{1,0:T(8,128)(2,1)S(1)} %bitcast.54), channel_id=1, source_target_pairs={{0,4},{4,8},{8,12},{12,16},{16,20},{20,24},{24,28},{28,32},{32,36}... | collective-permute-start | bytes 1572872 | tf_op jit(solution)/shard_map/ppermute | solution.py:12
  144.7 4.4 copy.29
  150.6 2.4 fusion.12
  156.0 83.0 %psum.23 = f32[512]{0:T(512)} all-reduce(f32[512]{0:T(512)S(1)} %get-tuple-element.33), channel_id=1, replica_groups=mesh['dom'=64,'rep'=4] {'dom','rep'}, use_global_device_ids=true, to_apply=%region_7.8 | all-reduce | flops 512 | bytes 4096 | tf_op jit(solution)/shard_map/psum | solution.py:78
  239.5 2.2 add_convert_fusion
  241.7 234.0 %all-reduce.3.cloned.1.call-done = (f32[512,512]{1,0:T(8,128)}, f32[512,512]{1,0:T(8,128)}) async-done(((f32[512,512]{1,0:T(8,128)}, f32[512,512]{1,0:T(8,128)}), (f32[512,512]{1,0:T(8,128)}, f32[512,512]{1,0:T(8,128)})) %all-reduce.3.cloned.1.call-update) | async-done | bytes 2097168 | tf_op jit(solution)/shard_map/psum | solution.py:78
  475.6 2.3 copy.44
  477.9 2.3 copy.45
  (68 shorter events, 18.5 us)
Async XLA Ops:
  7.2 108.7 %copy-start = (bf16[512,512]{1,0:T(8,128)(2,1)S(1)}, bf16[512,512]{1,0:T(8,128)(2,1)}, u32[]{:S(2)}) copy-start(bf16[512,512]{1,0:T(8,128)(2,1)} %param.19) | copy-start | bytes 1572868
  7.2 20.9 %copy-start.1 = (bf16[512,512]{1,0:T(8,128)(2,1)S(1)}, bf16[512,512]{1,0:T(8,128)(2,1)}, u32[]{:S(2)}) copy-start(bf16[512,512]{1,0:T(8,128)(2,1)} %param.13) | copy-start | bytes 1572868
  15.3 47.4 %copy-start.10 = (s32[4,12]{1,0:T(4,128)S(1)}, s32[4,12]{1,0:T(4,128)}, u32[]{:S(2)}) copy-start(s32[4,12]{1,0:T(4,128)} %param.16) | copy-start | bytes 580
  15.3 47.5 %copy-start.9 = (s32[4,12]{1,0:T(4,128)S(1)}, s32[4,12]{1,0:T(4,128)}, u32[]{:S(2)}) copy-start(s32[4,12]{1,0:T(4,128)} %param.17) | copy-start | bytes 580
  15.3 47.5 %copy-start.3 = (bf16[4,12,128,128]{3,2,1,0:T(8,128)(2,1)S(1)}, bf16[4,12,128,128]{3,2,1,0:T(8,128)(2,1)}, u32[]{:S(2)}) copy-start(bf16[4,12,128,128]{3,2,1,0:T(8,128)(2,1)} %param.15) | copy-start | bytes 4718596
  16.0 21.5 %all-to-all-start = ((s32[64,8,1]{1,2,0:T(1,128)}), s32[64,8,1]{1,2,0:T(1,128)S(1)}, u32[]{:S(2)}, u32[]{:S(2)}) async-start(s32[64,8,1]{1,2,0:T(1,128)} %bitcast), calls=%async_computation | async-start | bytes 65536 | tf_op jit(solution)/shard_map/all_to_all | solution.py:58
  30.7 67.8 %copy-start.4 = (bf16[512,512]{1,0:T(8,128)(2,1)S(1)}, bf16[512,512]{1,0:T(8,128)(2,1)}, u32[]{:S(2)}) copy-start(bf16[512,512]{1,0:T(8,128)(2,1)} %param.18) | copy-start | bytes 1572868
  37.5 21.8 %all-to-all-start.1 = ((bf16[64,8,512]{2,1,0:T(8,128)(2,1)}), bf16[64,8,512]{2,1,0:T(8,128)(2,1)S(1)}, u32[]{:S(2)}, u32[]{:S(2)}) async-start(bf16[64,8,512]{2,1,0:T(8,128)(2,1)} %bitcast.2), calls=%async_computation.1 | async-start | bytes 1048576 | tf_op jit(solution)/shard_map/all_to_all | solution.py:57
  42.2 50.2 %all-gather.2.cloned.1.call-start = ((), (), s32[]{:S(2)}) async-start(), calls=%async_computation.3 | async-start | bytes 2621440 | tf_op jit(solution)/shard_map/all_gather | solution.py:65
  62.5 36.0 %copy-start.2 = (bf16[512,512]{1,0:T(8,128)(2,1)S(1)}, bf16[512,512]{1,0:T(8,128)(2,1)}, u32[]{:S(2)}) copy-start(bf16[512,512]{1,0:T(8,128)(2,1)} %scatter_custom_fusion) | copy-start | bytes 1572868
  62.6 176.9 %reduce-scatter.2.cloned.1.call-start = ((), (), s32[]{:S(2)}) async-start(), calls=%async_computation.4 | async-start | bytes 5242880 | tf_op jit(solution)/shard_map/reduce_scatter | solution.py:106
  94.6 5.3 %collective-permute-start = (bf16[512,512]{1,0:T(8,128)(2,1)}, bf16[512,512]{1,0:T(8,128)(2,1)}, u32[]{:S(2)}, u32[]{:S(2)}) collective-permute-start(bf16[512,512]{1,0:T(8,128)(2,1)} %get-tuple-element.39), channel_id=1, source_target_pairs={{0,4},{4,8},{8,12},{12,16},{16,20},{20,24},{24,28},{28,32},{32,36}... | collective-permute-start | bytes 1572872 | tf_op jit(solution)/shard_map/ppermute | solution.py:20
  97.2 4.7 collective-permute-start.1
  111.8 4.1 copy-start.6
  111.9 4.1 copy-start.11
  111.9 4.1 copy-start.12
  115.9 2.3 copy-start.7
  132.9 16.5 %collective-permute-start.2 = (bf16[512,512]{1,0:T(8,128)(2,1)S(1)}, bf16[512,512]{1,0:T(8,128)(2,1)S(1)}, u32[]{:S(2)}, u32[]{:S(2)}) collective-permute-start(bf16[512,512]{1,0:T(8,128)(2,1)S(1)} %bitcast.54), channel_id=1, source_target_pairs={{0,4},{4,8},{8,12},{12,16},{16,20},{20,24},{24,28},{28,32},{32,36}... | collective-permute-start | bytes 1572872 | tf_op jit(solution)/shard_map/ppermute | solution.py:12
  142.1 8.5 %collective-permute-start.3 = (bf16[512,512]{1,0:T(8,128)(2,1)S(1)}, bf16[512,512]{1,0:T(8,128)(2,1)S(1)}, u32[]{:S(2)}, u32[]{:S(2)}) collective-permute-start(bf16[512,512]{1,0:T(8,128)(2,1)S(1)} %bitcast.53), channel_id=1, source_target_pairs={{4,0},{8,4},{12,8},{16,12},{20,16},{24,20},{28,24},{32,28},{36,32}... | collective-permute-start | bytes 1572872 | tf_op jit(solution)/shard_map/ppermute | solution.py:12
  149.5 3.7 copy-start.8
  153.1 85.9 %copy-start.5 = (bf16[512,512]{1,0:T(8,128)(2,1)S(1)}, bf16[512,512]{1,0:T(8,128)(2,1)}, u32[]{:S(2)}) copy-start(bf16[512,512]{1,0:T(8,128)(2,1)} %param.18) | copy-start | bytes 1572868
  153.1 322.6 %all-reduce.3.cloned.1.call-start = ((), (), s32[]{:S(2)}) async-start(), calls=%async_computation.5 | async-start | bytes 4194304 | tf_op jit(solution)/shard_map/psum | solution.py:78
Sparse Core Ops, SparseCore 0:
  62.7 29.6 all-gather.1
  153.2 52.8 reduce-scatter.1
  213.1 262.4 all-reduce.2
where the time goes:
time: 487 us
  waiting for transfers between devices  288 us (59%)
  blocking collectives  83 us (17%)
  local copies, waits for them, and re-layouts  31.1 us (6%)
  starting transfers between devices  31.1 us (6%)
  matrix products  25.2 us (5%)
  other arithmetic  14.6 us (3%)
  between operations  14.1 us (3%)
    psum x1, waiting for transfers between devices, shards(): lax.psum((contract_rows(features, dz), contract_rows(agg, dz), jnp.sum(dz...  234 us
    psum x1, blocking collectives, shards(): lax.psum((contract_rows(features, dz), contract_rows(agg, dz), jnp.sum(dz...  83 us
    all_gather x1, waiting for transfers between devices, shards(): whole = lax.all_gather(features, 'rep', axis=0, tiled=True)  29.2 us
    all_to_all x1, waiting for transfers between devices, shards(): lax.all_to_all(x_loader[order], 'dom', split_axis=0, concat_axis=0, tiled...  15.8 us
    dot_general x1, matrix products, shards(): jnp.einsum('en,nbf->ebf', selector, terms.reshape(-1, 128, width), precis...  12.3 us
    all_to_all x1, starting transfers between devices, shards(): lax.all_to_all((owner_index % rows)[order], 'dom', split_axis=0, concat_a...  12.1 us
    ppermute x2, starting transfers between devices, shifted(): lax.ppermute(value, axis, [(source, source + steps) for source in range(f...  10.4 us
  transfers between devices with their start and end apart: 9, of which 5 were waited for; matrix products, arithmetic and copies ran while one was open for 4% of the time, Pallas kernels for 0%

commit v1 on v0

--- a/solution.py
+++ b/solution.py
@@ -62,7 +62,15 @@
     local_cols = tile_cols - first_tile
     masked = tile_vals * tile_live.astype(jnp.bfloat16)[:, :, None, None]
     degree = 1.0 + jnp.sum(masked, axis=(1, 3), dtype=jnp.float32)
-    whole = lax.all_gather(features, "rep", axis=0, tiled=True)
+    devices = lax.axis_size("rep")
+    block_2, pieces = (features, [features])
+    for _ in range(devices - 1):
+        block_2 = lax.ppermute(
+            block_2, "rep", [(i_2, (i_2 + 1) % devices) for i_2 in range(devices)]
+        )
+        pieces.insert(0, block_2)
+    line = jnp.concatenate(pieces, axis=0)
+    whole = jnp.roll(line, (lax.axis_index("rep") + 1) * features.shape[0], axis=0)
     extended = with_halo(whole, (("dom", 0),), rim_rows)
     picked = extended.reshape(-1, 128, width)[local_cols]
     summed = jnp.einsum("tkab,tkbf->taf", masked, picked, preferred_element_type=jnp.float32)

time: 487 us -> 465 us (0.955)
  waiting for transfers between devices: 288 us -> 258 us
    ppermute x0 -> x3, waiting for transfers between devices: none -> 35.6 us  [shards(): lax.ppermute(block_2, 'rep', [(i_2, (i_2 + 1) % devices) for i_2 in range...]
    psum x1, waiting for transfers between devices: 234 us -> 198 us  [shards(): lax.psum((contract_rows(features, dz), contract_rows(agg, dz), jnp.sum(dz...]
    all_gather x1 -> x0, waiting for transfers between devices: 29.2 us -> none  [shards(): whole = lax.all_gather(features, 'rep', axis=0, tiled=True)]
  transfers between devices with their start and end apart: 9 -> 11, of which waited for: 5 -> 7; matrix products, arithmetic and copies ran while one was open for 4% -> 4% of each run, Pallas kernels for 0% -> 0%
where the time goes in v1:
time: 465 us; the launch traced here: 464 us
  waiting for transfers between devices  258 us (55%)
  blocking collectives  86.1 us (19%)
  starting transfers between devices  34.4 us (7%)
  local copies, waits for them, and re-layouts  31.3 us (7%)
  matrix products  25.2 us (5%)
  between operations  15.9 us (3%)
  other arithmetic  13.3 us (3%)
    psum x1, waiting for transfers between devices, shards(): lax.psum((contract_rows(features, dz), contract_rows(agg, dz), jnp.sum(dz...  198 us
    psum x1, blocking collectives, shards(): lax.psum((contract_rows(features, dz), contract_rows(agg, dz), jnp.sum(dz...  86.1 us
    ppermute x3, waiting for transfers between devices, shards(): lax.ppermute(block_2, 'rep', [(i_2, (i_2 + 1) % devices) for i_2 in range...  35.6 us
    all_to_all x1, waiting for transfers between devices, shards(): lax.all_to_all(x_loader[order], 'dom', split_axis=0, concat_axis=0, tiled...  15.8 us
    dot_general x1, matrix products, shards(): jnp.einsum('en,nbf->ebf', selector, terms.reshape(-1, 128, width), precis...  12.3 us
    all_to_all x1, starting transfers between devices, shards(): lax.all_to_all((owner_index % rows)[order], 'dom', split_axis=0, concat_a...  12.1 us
    ppermute x2, starting transfers between devices, shifted(): lax.ppermute(value, axis, [(source, source + steps) for source in range(f...  10.4 us
  transfers between devices with their start and end apart: 11, of which 7 were waited for; matrix products, arithmetic and copies ran while one was open for 4% of the time, Pallas kernels for 0%

profile of v1, /device:TPU:2, one launch (start us, length us, event | category | flops | bytes accessed | tf_op | source)
XLA Modules:
  0.0 464.4 jit_solution(15698030069344955255)
XLA Ops:
  8.8 3.8 sort.17
  12.6 3.5 gather_fusion
  16.8 12.1 %all-to-all-start = ((s32[64,8,1]{1,2,0:T(1,128)}), s32[64,8,1]{1,2,0:T(1,128)S(1)}, u32[]{:S(2)}, u32[]{:S(2)}) async-start(s32[64,8,1]{1,2,0:T(1,128)} %bitcast), calls=%async_computation | async-start | bytes 65536 | tf_op jit(solution)/shard_map/all_to_all | solution.py:58
  28.9 2.6 gather_fusion.1
  31.6 6.8 %all-to-all-done = s32[64,8,1]{1,2,0:T(1,128)S(1)} async-done(((s32[64,8,1]{1,2,0:T(1,128)}), s32[64,8,1]{1,2,0:T(1,128)S(1)}, u32[]{:S(2)}, u32[]{:S(2)}) %all-to-all-start) | async-done | bytes 2080 | tf_op jit(solution)/shard_map/all_to_all | solution.py:58
  38.4 4.6 all-to-all-start.1
  44.4 15.8 %all-to-all-done.1 = bf16[64,8,512]{2,1,0:T(8,128)(2,1)S(1)} async-done(((bf16[64,8,512]{2,1,0:T(8,128)(2,1)}), bf16[64,8,512]{2,1,0:T(8,128)(2,1)S(1)}, u32[]{:S(2)}, u32[]{:S(2)}) %all-to-all-start.1) | async-done | bytes 524320 | tf_op jit(solution)/shard_map/all_to_all | solution.py:57
  60.2 2.5 scatter_custom_fusion
  64.3 12.5 %collective-permute-done = bf16[512,512]{1,0:T(8,128)(2,1)S(1)} collective-permute-done((bf16[512,512]{1,0:T(8,128)(2,1)S(1)}, bf16[512,512]{1,0:T(8,128)(2,1)S(1)}, u32[]{:S(2)}, u32[]{:S(2)}) %collective-permute-start) | collective-permute-done | bytes 524320 | tf_op jit(solution)/shard_map/ppermute | solution.py:68
  78.4 11.5 %collective-permute-done.1 = bf16[512,512]{1,0:T(8,128)(2,1)} collective-permute-done((bf16[512,512]{1,0:T(8,128)(2,1)S(1)}, bf16[512,512]{1,0:T(8,128)(2,1)}, u32[]{:S(2)}, u32[]{:S(2)}) %collective-permute-start.1) | collective-permute-done | bytes 524320 | tf_op jit(solution)/shard_map/ppermute | solution.py:68
  91.9 11.6 %collective-permute-done.2 = bf16[512,512]{1,0:T(8,128)(2,1)S(1)} collective-permute-done((bf16[512,512]{1,0:T(8,128)(2,1)}, bf16[512,512]{1,0:T(8,128)(2,1)S(1)}, u32[]{:S(2)}, u32[]{:S(2)}) %collective-permute-start.2) | collective-permute-done | bytes 524320 | tf_op jit(solution)/shard_map/ppermute | solution.py:68
  112.3 1.8 pad_maximum_fusion
  114.1 6.8 %gather_fusion.2 = bf16[48,128,512]{2,1,0:T(8,128)(2,1)} fusion(bf16[24,128,512]{2,1,0:T(8,128)(2,1)} %bitcast.50, s32[1024]{0:T(1024)S(1)} %pad_clamp_fusion), kind=kCustom, calls=%fused_computation.2 | custom fusion | bytes 12583104 | tf_op jit(solution)/shard_map/gather | solution.py:75
  120.9 4.0 fusion.5
  127.2 1.9 fusion.6
  129.1 12.3 %fusion.26 = (bf16[24,128,512]{2,0,1:T(8,128)(2,1)S(1)}, f32[24,128,512]{2,0,1:T(8,128)S(1)}) fusion(f32[48,128,512]{2,1,0:T(8,128)S(1)} %bitcast.49, s32[48]{0:T(128)S(1)} %eq.20), kind=kOutput, calls=%fused_computation.66 | convolution fusion | flops 907543680 | bytes 22020288 | tf_op jit(solution)/shard_map/en,nbf->ebf/dot_general | solution.py:105
  142.0 9.1 %collective-permute-start.5 = (bf16[512,512]{1,0:T(8,128)(2,1)S(1)}, bf16[512,512]{1,0:T(8,128)(2,1)S(1)}, u32[]{:S(2)}, u32[]{:S(2)}) collective-permute-start(bf16[512,512]{1,0:T(8,128)(2,1)S(1)} %bitcast.54), channel_id=1, source_target_pairs={{0,4},{4,8},{8,12},{12,16},{16,20},{20,24},{24,28},{28,32},{32,36}... | collective-permute-start | bytes 1572872 | tf_op jit(solution)/shard_map/ppermute | solution.py:12
  153.8 4.4 copy.29
  159.7 2.4 fusion.12
  165.1 86.1 %psum.23 = f32[512]{0:T(512)} all-reduce(f32[512]{0:T(512)S(1)} %get-tuple-element.33), channel_id=1, replica_groups=mesh['dom'=64,'rep'=4] {'dom','rep'}, use_global_device_ids=true, to_apply=%region_7.8 | all-reduce | flops 512 | bytes 4096 | tf_op jit(solution)/shard_map/psum | solution.py:86
  251.8 2.2 add_convert_fusion
  253.9 198.5 %all-reduce.3.cloned.1.call-done = (f32[512,512]{1,0:T(8,128)}, f32[512,512]{1,0:T(8,128)}) async-done(((f32[512,512]{1,0:T(8,128)}, f32[512,512]{1,0:T(8,128)}), (f32[512,512]{1,0:T(8,128)}, f32[512,512]{1,0:T(8,128)})) %all-reduce.3.cloned.1.call-update) | async-done | bytes 2097168 | tf_op jit(solution)/shard_map/psum | solution.py:86
  452.4 2.3 copy.51
  454.7 2.3 copy.52
  (80 shorter events, 27.0 us)
Async XLA Ops:
  8.0 117.0 %copy-start = (bf16[512,512]{1,0:T(8,128)(2,1)S(1)}, bf16[512,512]{1,0:T(8,128)(2,1)}, u32[]{:S(2)}) copy-start(bf16[512,512]{1,0:T(8,128)(2,1)} %param.19) | copy-start | bytes 1572868
  8.0 20.9 %copy-start.2 = (bf16[512,512]{1,0:T(8,128)(2,1)S(1)}, bf16[512,512]{1,0:T(8,128)(2,1)}, u32[]{:S(2)}) copy-start(bf16[512,512]{1,0:T(8,128)(2,1)} %param.13) | copy-start | bytes 1572868
  12.6 65.7 %copy-start.10 = (s32[4,12]{1,0:T(4,128)S(1)}, s32[4,12]{1,0:T(4,128)}, u32[]{:S(2)}) copy-start(s32[4,12]{1,0:T(4,128)} %param.16) | copy-start | bytes 580
  12.6 65.7 %copy-start.9 = (s32[4,12]{1,0:T(4,128)S(1)}, s32[4,12]{1,0:T(4,128)}, u32[]{:S(2)}) copy-start(s32[4,12]{1,0:T(4,128)} %param.17) | copy-start | bytes 580
  12.6 78.8 %copy-start.3 = (bf16[4,12,128,128]{3,2,1,0:T(8,128)(2,1)S(1)}, bf16[4,12,128,128]{3,2,1,0:T(8,128)(2,1)}, u32[]{:S(2)}) copy-start(bf16[4,12,128,128]{3,2,1,0:T(8,128)(2,1)} %param.15) | copy-start | bytes 4718596
  16.8 21.5 %all-to-all-start = ((s32[64,8,1]{1,2,0:T(1,128)}), s32[64,8,1]{1,2,0:T(1,128)S(1)}, u32[]{:S(2)}, u32[]{:S(2)}) async-start(s32[64,8,1]{1,2,0:T(1,128)} %bitcast), calls=%async_computation | async-start | bytes 65536 | tf_op jit(solution)/shard_map/all_to_all | solution.py:58
  38.4 21.8 %all-to-all-start.1 = ((bf16[64,8,512]{2,1,0:T(8,128)(2,1)}), bf16[64,8,512]{2,1,0:T(8,128)(2,1)S(1)}, u32[]{:S(2)}, u32[]{:S(2)}) async-start(bf16[64,8,512]{2,1,0:T(8,128)(2,1)} %bitcast.2), calls=%async_computation.1 | async-start | bytes 1048576 | tf_op jit(solution)/shard_map/all_to_all | solution.py:57
  43.0 208.8 %reduce-scatter.2.cloned.1.call-start = ((), (), s32[]{:S(2)}) async-start(), calls=%async_computation.3 | async-start | bytes 5242880 | tf_op jit(solution)/shard_map/reduce_scatter | solution.py:114
  62.7 14.0 %collective-permute-start = (bf16[512,512]{1,0:T(8,128)(2,1)S(1)}, bf16[512,512]{1,0:T(8,128)(2,1)S(1)}, u32[]{:S(2)}, u32[]{:S(2)}) collective-permute-start(bf16[512,512]{1,0:T(8,128)(2,1)S(1)} %scatter_custom_fusion), channel_id=1, source_target_pairs={{0,1},{1,2},{2,3},{3,0},{4,5},{5,6},{6,7},{7,4},{8,9},{9,10},{10,1... | collective-permute-start | bytes 1572872 | tf_op jit(solution)/shard_map/ppermute | solution.py:68
  76.7 13.2 %collective-permute-start.1 = (bf16[512,512]{1,0:T(8,128)(2,1)S(1)}, bf16[512,512]{1,0:T(8,128)(2,1)}, u32[]{:S(2)}, u32[]{:S(2)}) collective-permute-start(bf16[512,512]{1,0:T(8,128)(2,1)S(1)} %collective-permute-done), channel_id=1, source_target_pairs={{0,1},{1,2},{2,3},{3,0},{4,5},{5,6},{6,7},{7,4},{8,9},{9,10},{10,1... | collective-permute-start | bytes 1572872 | tf_op jit(solution)/shard_map/ppermute | solution.py:68
  90.0 13.6 %collective-permute-start.2 = (bf16[512,512]{1,0:T(8,128)(2,1)}, bf16[512,512]{1,0:T(8,128)(2,1)S(1)}, u32[]{:S(2)}, u32[]{:S(2)}) collective-permute-start(bf16[512,512]{1,0:T(8,128)(2,1)} %collective-permute-done.1), channel_id=1, source_target_pairs={{0,1},{1,2},{2,3},{3,0},{4,5},{5,6},{6,7},{7,4},{8,9},{9,10},{10,1... | collective-permute-start | bytes 1572872 | tf_op jit(solution)/shard_map/ppermute | solution.py:68
  104.7 4.2 copy-start.4
  106.3 4.6 collective-permute-start.3
  107.6 4.6 collective-permute-start.4
  120.9 4.1 copy-start.6
  120.9 4.1 copy-start.11
  120.9 4.1 copy-start.12
  124.9 2.3 copy-start.7
  142.0 16.6 %collective-permute-start.5 = (bf16[512,512]{1,0:T(8,128)(2,1)S(1)}, bf16[512,512]{1,0:T(8,128)(2,1)S(1)}, u32[]{:S(2)}, u32[]{:S(2)}) collective-permute-start(bf16[512,512]{1,0:T(8,128)(2,1)S(1)} %bitcast.54), channel_id=1, source_target_pairs={{0,4},{4,8},{8,12},{12,16},{16,20},{20,24},{24,28},{28,32},{32,36}... | collective-permute-start | bytes 1572872 | tf_op jit(solution)/shard_map/ppermute | solution.py:12
  151.2 8.5 %collective-permute-start.6 = (bf16[512,512]{1,0:T(8,128)(2,1)S(1)}, bf16[512,512]{1,0:T(8,128)(2,1)S(1)}, u32[]{:S(2)}, u32[]{:S(2)}) collective-permute-start(bf16[512,512]{1,0:T(8,128)(2,1)S(1)} %bitcast.53), channel_id=1, source_target_pairs={{4,0},{8,4},{12,8},{16,12},{20,16},{24,20},{28,24},{32,28},{36,32}... | collective-permute-start | bytes 1572872 | tf_op jit(solution)/shard_map/ppermute | solution.py:12
  159.7 2.5 copy-start.8
  162.2 89.1 %copy-start.5 = (bf16[512,512]{1,0:T(8,128)(2,1)S(1)}, bf16[512,512]{1,0:T(8,128)(2,1)}, u32[]{:S(2)}) copy-start(bf16[512,512]{1,0:T(8,128)(2,1)} %param.18) | copy-start | bytes 1572868
  162.2 290.2 %all-reduce.3.cloned.1.call-start = ((), (), s32[]{:S(2)}) async-start(), calls=%async_computation.4 | async-start | bytes 4194304 | tf_op jit(solution)/shard_map/psum | solution.py:86
  165.1 291.8 %copy-start.1 = (bf16[512,512]{1,0:T(8,128)(2,1)S(1)}, bf16[512,512]{1,0:T(8,128)(2,1)}, u32[]{:S(2)}) copy-start(bf16[512,512]{1,0:T(8,128)(2,1)} %param.19) | copy-start | bytes 1572868
Sparse Core Ops, SparseCore 0:
  162.3 55.4 reduce-scatter.1
Sparse Core Ops, SparseCore 1:
  169.7 282.7 all-reduce.2
